TPU v7x, 512 devices: a whole 4x8x8 slice. The times are simulated.
512 devices in a mesh: grp: 16 (over z, core), dev: 32 (over x, y).
Axes of the slice: x: 4, y: 8, z: 8, core: 2. Of those that a mesh axis runs over, the one named last changes fastest.
Arguments:
- ssm_input: bfloat16 [4096, 4096], P('grp', 'dev'), may hold values from -6 to 6
- gate_input: bfloat16 [4096, 4096], P('grp', 'dev'), may hold values from -6 to 6
- step_size: float32 [4096, 64], P('grp', 'dev'), may hold values from 6.1035156e-05 to 0.3375
- decay_rate: float32 [64], P('dev'), may hold values from 0.5 to 2
- in_coeff: bfloat16 [4096, 128], P('grp'), may hold values from -6 to 6
- out_coeff: bfloat16 [4096, 128], P('grp'), may hold values from -6 to 6
- skip_gain: float32 [64], P('dev'), may hold values from 0.5 to 3
- norm_gain: float32 [4096], P('dev'), may hold values from 0.5 to 1.5
- out_proj: bfloat16 [4096, 2048], P(None, 'dev'), may hold values from -0.09375 to 0.09375
- residual: bfloat16 [4096, 2048], P(('grp', 'dev')), may hold values from -6 to 6
- ffn_gain: float32 [2048], replicated, may hold values from 0.5 to 1.5
- router: float32 [2048, 16], replicated, may hold values from -0.125 to 0.125
- routes: int32 [4096, 2], P(('grp', 'dev')), may hold values from 0 to 15, all different within a row; in each aligned block of 8 rows (0 to 7, 8 to 15, ...) at most 2 rows name the same one
- gate_weight: bfloat16 [16, 2048, 8192], P('grp', None, 'dev'), may hold values from -0.125 to 0.125
- up_weight: bfloat16 [16, 2048, 8192], P('grp', None, 'dev'), may hold values from -0.125 to 0.125
- down_weight: bfloat16 [16, 8192, 2048], P('grp', 'dev'), may hold values from -0.0625 to 0.0625
Outputs:
- moe_out: bfloat16 [4096, 2048], P(('grp', 'dev'))
Inputs may be any that keep to these rules, and one draw needn't show every extreme that they name: `routes`: each row names two different experts; among the 8 rows of one dispatch block of consecutive tokens no expert is named more than 2 times, a bound that some block reaches.
All inputs are finite; a program needn't handle non-finite values.
Results may differ from a plain program's by a relative error of at most 0.012.
Values may be sent and summed in bfloat16 or wider, within the bound.
No kernel may reach another device: no remote copies, remote signals or barrier semaphores. Data moves between devices by JAX's collectives and lax.ppermute only.
A program may use at most 64 MiB of HBM per device.

v0:
```python
import jax
import jax.numpy as jnp
from jax import lax
from jax.sharding import Mesh
from jax.sharding import PartitionSpec as P

DEV = ("dev_0", "dev_1")
GRP_DEV = ("grp", "dev_0", "dev_1")
EPSILON = 1e-05
HIGHEST_PREC = lax.Precision.HIGHEST


def side_by_side(arrays, axis, dim, along):
    columns = [a.reshape(*a.shape[:along], -1) for a in arrays]
    both = jnp.concatenate(columns, axis=along)
    filled, at, finished = (lax.all_gather(both, axis, axis=dim, tiled=True), 0, [])
    for a, column in zip(arrays, columns):
        piece = filled[..., at : at + column.shape[along]]
        finished.append(piece.reshape(*piece.shape[:along], *a.shape[along:]))
        at += column.shape[along]
    return tuple(finished)


def sent_to_all(shard, axis):
    peers = lax.axis_size(axis)
    return lax.all_to_all(
        jnp.broadcast_to(shard[None], (peers, *shard.shape)), axis, 0, 0, tiled=True
    )


def of_everyone(shard, axis):
    everything = sent_to_all(shard, axis)
    return jnp.sum(everything, axis=0)


def in_order(tiles, dim):
    dims = list(tiles.shape[1:])
    dims[dim] *= tiles.shape[0]
    return jnp.moveaxis(tiles, 0, dim).reshape(dims)


def collect(shard, axis, dim):
    return in_order(sent_to_all(shard, axis), dim)


def sum_by_axis(terms, axes):
    total = terms.astype(jnp.bfloat16)
    total = lax.psum_scatter(total, axes, scatter_dimension=0, tiled=True)
    return total.astype(jnp.float32)


def rms_scale(values, gain_vec):
    return (
        values * lax.rsqrt(jnp.mean(values * values, axis=-1, keepdims=True) + EPSILON) * gain_vec
    )


def slot_tables(routes_block, expert_count, slot_cap):
    blocks, row_total = (routes_block.shape[0], routes_block.shape[1])
    flat_routes = routes_block.reshape(blocks, row_total * 2)
    onehot = (
        flat_routes[:, :, None] == jnp.arange(expert_count, dtype=jnp.int32)[None, None, :]
    ).astype(jnp.int32)
    earlier = jnp.cumsum(onehot, axis=1) - onehot
    slot_rank = jnp.sum(earlier * onehot, axis=2)
    slot_index = (flat_routes * slot_cap + slot_rank).reshape(blocks, row_total, 2)
    placed = (
        slot_index[:, :, :, None]
        == jnp.arange(expert_count * slot_cap, dtype=jnp.int32)[None, None, None, :]
    )
    return placed.astype(jnp.float32)


def shards(
    ssm_input,
    gate_input,
    step_size,
    decay_rate,
    in_coeff,
    out_coeff,
    skip_gain,
    norm_gain,
    out_proj,
    residual,
    ffn_gain,
    router,
    routes,
    gate_weight,
    up_weight,
    down_weight,
):
    tok_rows = ssm_input.shape[0]
    head_count = step_size.shape[1]
    head_width = ssm_input.shape[1] // head_count
    dev_count = lax.axis_size(DEV)
    inner_dim = ssm_input.shape[1] * dev_count
    block_rows = residual.shape[0]
    model_dim = residual.shape[1]
    experts = lax.axis_size("grp")
    slot_cap = max(2, 4 * block_rows // experts)
    group_slots = experts * slot_cap
    inputs_f = ssm_input.astype(jnp.float32).reshape(tok_rows, head_count, head_width)
    in_float = in_coeff.astype(jnp.float32)
    out_float = out_coeff.astype(jnp.float32)
    log_rate = -(step_size * decay_rate[None, :])
    cumulative = jnp.cumsum(log_rate, axis=0)
    causal = (jnp.arange(tok_rows)[:, None] >= jnp.arange(tok_rows)[None, :])[:, :, None]
    spread = cumulative[:, None, :] - cumulative[None, :, :]
    decay_pair = jnp.where(causal, jnp.exp(jnp.where(causal, spread, 0.0)), 0.0)
    scores = jnp.dot(out_coeff, in_coeff.T, preferred_element_type=jnp.float32)
    mixing = decay_pair * scores[:, :, None] * step_size[None, :, :]
    inside = jnp.einsum("tuh,uhp->thp", mixing, inputs_f, precision=HIGHEST_PREC)
    to_end = jnp.exp(cumulative[-1][None, :] - cumulative) * step_size
    own_state = jnp.einsum("uh,uhp,un->hpn", to_end, inputs_f, in_float, precision=HIGHEST_PREC)
    own_log = cumulative[-1]
    group_logs, group_states = tuple(
        (
            part.astype(jnp.float32)
            for part in side_by_side(
                (own_log[None].astype(jnp.bfloat16), own_state[None].astype(jnp.bfloat16)),
                "grp",
                0,
                2,
            )
        )
    )
    group_index = jnp.arange(group_logs.shape[0])
    my_group = lax.axis_index("grp")
    inclusive = jnp.cumsum(group_logs, axis=0)
    exclusive = inclusive - group_logs
    before_me = jnp.sum(jnp.where((group_index == my_group)[:, None], exclusive, 0.0), axis=0)
    earlier_mask = (group_index < my_group)[:, None]
    weighting = jnp.where(
        earlier_mask, jnp.exp(jnp.where(earlier_mask, before_me[None, :] - inclusive, 0.0)), 0.0
    )
    entering = jnp.einsum("gh,ghpn->hpn", weighting, group_states, precision=HIGHEST_PREC)
    carried = jnp.exp(cumulative)[:, :, None] * jnp.einsum(
        "hpn,tn->thp", entering, out_float, precision=HIGHEST_PREC
    )
    ssm_out = inside + carried + skip_gain[None, :, None] * inputs_f
    gated_out = ssm_out.reshape(tok_rows, head_count * head_width) * jax.nn.silu(
        gate_input.astype(jnp.float32)
    )
    squares = lax.psum(jnp.sum(gated_out * gated_out, axis=1), DEV)
    mixed_rows = (
        gated_out * lax.rsqrt(squares[:, None] / inner_dim + EPSILON) * norm_gain[None, :]
    ).astype(jnp.bfloat16)
    gathered = lax.all_gather(mixed_rows, DEV, axis=0)
    projected = jnp.einsum(
        "dtc,dcf->tf",
        gathered,
        out_proj.reshape(dev_count, -1, out_proj.shape[1]),
        preferred_element_type=jnp.float32,
    ).astype(jnp.bfloat16)
    mamba_out = lax.all_to_all(projected, DEV, split_axis=0, concat_axis=1, tiled=True)
    hidden_res = (residual.astype(jnp.float32) + mamba_out.astype(jnp.float32)).astype(jnp.bfloat16)
    hidden_float = hidden_res.astype(jnp.float32)
    normed = rms_scale(hidden_float, ffn_gain).astype(jnp.bfloat16)
    logits = jnp.dot(normed.astype(jnp.float32), router, precision=HIGHEST_PREC)
    expert_ids = jnp.arange(experts, dtype=jnp.int32)[None, :]
    first_logit = jnp.sum(logits * (routes[:, 0:1] == expert_ids).astype(jnp.float32), axis=1)
    second_logit = jnp.sum(logits * (routes[:, 1:2] == expert_ids).astype(jnp.float32), axis=1)
    first_prob = jax.nn.sigmoid(first_logit - second_logit)
    second_prob = 1.0 - first_prob
    placed = slot_tables(routes[None], experts, slot_cap)[0]
    filled = jnp.sum(placed, axis=1)
    outgoing = jnp.dot(
        filled.T.astype(jnp.bfloat16), normed, preferred_element_type=jnp.float32
    ).astype(jnp.bfloat16)
    outgoing = outgoing.reshape(experts, slot_cap, model_dim)
    arrived = lax.all_to_all(outgoing, "grp", split_axis=0, concat_axis=0, tiled=True)
    all_rows = lax.all_gather(arrived, DEV, axis=0, tiled=True).reshape(-1, model_dim)
    gate_act = jnp.dot(all_rows, gate_weight[0], preferred_element_type=jnp.float32)
    up_act = jnp.dot(all_rows, up_weight[0], preferred_element_type=jnp.float32)
    hidden = (jax.nn.silu(gate_act) * up_act).astype(jnp.bfloat16)
    summed = sum_by_axis(jnp.dot(hidden, down_weight[0], preferred_element_type=jnp.float32), DEV)
    returned = lax.all_to_all(
        summed.astype(jnp.bfloat16).reshape(experts, slot_cap, model_dim),
        "grp",
        split_axis=0,
        concat_axis=0,
        tiled=True,
    )
    weights = first_prob[:, None] * placed[:, 0, :] + second_prob[:, None] * placed[:, 1, :]
    contrib = jnp.dot(
        weights,
        returned.reshape(group_slots, model_dim).astype(jnp.float32),
        precision=HIGHEST_PREC,
    )
    return (hidden_float + contrib).astype(jnp.bfloat16)


def solution(mesh):
    torus = Mesh(mesh.devices.reshape(mesh.shape["grp"], 4, 8), ("grp", "dev_0", "dev_1"))
    in_specs = (
        P("grp", DEV),
        P("grp", DEV),
        P("grp", DEV),
        P(DEV),
        P("grp", None),
        P("grp", None),
        P(DEV),
        P(DEV),
        P(None, DEV),
        P(GRP_DEV, None),
        P(),
        P(),
        P(GRP_DEV, None),
        P("grp", None, DEV),
        P("grp", None, DEV),
        P("grp", DEV, None),
    )
    out_specs = P(GRP_DEV, None)
    return jax.shard_map(
        shards, mesh=torus, in_specs=in_specs, out_specs=out_specs, check_vma=False
    )
```

profile of v0, /device:TPU:1, one launch (start us, length us, event | category | flops | bytes accessed | tf_op | source)
XLA Modules:
  0.0 574.6 jit_solution(1486846018110611630)
XLA Ops:
  6.6 0.9 negate_bitcast_fusion
  7.5 0.6 reduce-window.6
  8.1 0.2 slice_reduce_fusion
  8.3 0.2 reduce-window.9
  8.5 0.2 slice_reduce_fusion.1
  8.8 0.8 fusion.58
  9.5 0.9 copy.61
  10.5 1.0 convolution_convert_fusion.2
  11.6 0.1 pad_maximum_fusion
  11.7 26.0 %all_gather.12 = bf16[16,2,8193]{2,1,0:T(2,128)(2,1)S(1)} all-gather(bf16[1,2,8193]{2,1,0:T(2,128)(2,1)S(1)} %pad_maximum_fusion), channel_id=1, replica_groups=mesh['grp'=16,'dev_0'=4,'dev_1'=8] {'grp'}, dimensions={0}, use_global_device_ids=true | all-gather | bytes 557124 | tf_op jit(solution)/shard_map/all_gather | solution.py:16
  37.6 0.7 slice.40
  38.4 0.1 copy.76
  38.5 0.1 copy.64
  38.6 0.1 select_reduce_fusion.1
  38.8 0.1 copy.73
  38.9 0.4 reshape.234
  39.3 1.1 fusion.59
  40.3 0.6 fusion.18
  40.9 0.2 fusion.4
  41.2 0.6 fusion.3
  41.8 0.1 copy.66
  41.9 0.1 multiply_reduce_fusion
  42.0 61.3 %psum.7 = f32[256]{0:T(256)S(1)} all-reduce(f32[256]{0:T(256)S(1)} %multiply_reduce_fusion), channel_id=1, replica_groups=mesh['grp'=16,'dev_0'=4,'dev_1'=8] {'dev_0','dev_1'}, use_global_device_ids=true, to_apply=%region_5.6 | all-reduce | flops 256 | bytes 2048 | tf_op jit(solution)/shard_map/psum | solution.py:144
  103.4 0.7 multiply_convert_fusion
  104.4 0.2 select_reduce_fusion
  104.7 0.1 copy.72
  104.7 81.8 %all-gather.6.cloned.1.call-done = bf16[8192,128]{1,0:T(8,128)(2,1)} async-done(((bf16[256,128]{1,0:T(8,128)(2,1)}), bf16[8192,128]{1,0:T(8,128)(2,1)}) %all-gather.6.cloned.1.call-update) | async-done | bytes 2097168 | tf_op jit(solution)/shard_map/all_gather | solution.py:148
  186.6 2.3 fusion.5
  188.9 0.1 copy.68
  189.1 0.7 reshape.251
  189.8 4.9 all-to-all-start
  194.9 8.6 %all-to-all-done = bf16[32,2,256]{2,1,0:T(2,128)(2,1)S(1)} async-done(((bf16[32,2,256]{2,1,0:T(2,128)(2,1)}), bf16[32,2,256]{2,1,0:T(2,128)(2,1)S(1)}, u32[]{:S(2)}, u32[]{:S(2)}) %all-to-all-start) | async-done | bytes 32800 | tf_op jit(solution)/shard_map/all_to_all | solution.py:155
  203.5 0.1 reshape.252
  203.7 0.1 reshape.242
  203.8 0.1 fusion.37
  203.9 0.2 convolution_convert_fusion.1
  204.2 0.1 reshape.237
  204.3 22.8 %all_to_all.23 = bf16[16,2,2048]{2,1,0:T(2,128)(2,1)} all-to-all(bf16[16,2,2048]{2,1,0:T(2,128)(2,1)S(1)} %reshape.237), channel_id=1, replica_groups=mesh['grp'=16,'dev_0'=4,'dev_1'=8] {'grp'}, dimensions={0} | all-to-all | bytes 262144 | tf_op jit(solution)/shard_map/all_to_all | solution.py:171
  227.1 73.9 %all-gather.4.cloned.1.call-done = bf16[512,2,2048]{2,1,0:T(2,128)(2,1)} async-done(((bf16[16,2,2048]{2,1,0:T(2,128)(2,1)}), bf16[512,2,2048]{2,1,0:T(2,128)(2,1)}) %all-gather.4.cloned.1.call-update) | async-done | bytes 4194320 | tf_op jit(solution)/shard_map/all_gather | solution.py:172
  301.0 7.2 %reshape.238 = bf16[1024,2048]{1,0:T(8,128)(2,1)} reshape(bf16[512,2,2048]{2,1,0:T(2,128)(2,1)} %all-gather.4.cloned.1.call-done) | data formatting | bytes 8388608 | tf_op jit(solution)/shard_map/reshape | solution.py:172
  308.2 4.5 fusion.9
  312.8 9.1 %convolution_convert_fusion = bf16[1024,2048]{1,0:T(8,128)(2,1)} fusion(bf16[1024,2048]{1,0:T(8,128)(2,1)} %reshape.238, bf16[1,256,2048]{2,1,0:T(8,128)(2,1)S(1)} %copy-done, bf16[1,2048,256]{2,1,0:T(8,128)(2,1)} %param.30, f32[1024,256]{1,0:T(8,128)} %fusion.9), kind=kOutput, calls=%fused_computation | convolution fusion | flops 2151153664 | bytes 11534336 | tf_op jit(solution)/shard_map/dot_general | solution.py:176
  322.0 222.0 %reduce-scatter.2.cloned.1.call-done = bf16[32,2048]{1,0:T(8,128)(2,1)} async-done(((bf16[1024,2048]{1,0:T(8,128)(2,1)}), bf16[32,2048]{1,0:T(8,128)(2,1)}) %reduce-scatter.2.cloned.1.call-update) | async-done | bytes 131088 | tf_op jit(solution)/shard_map/reduce_scatter | solution.py:48
  544.0 1.7 reshape.239
  545.6 12.4 %all-to-all-start.2 = ((bf16[16,2,2048]{2,1,0:T(2,128)(2,1)}), bf16[16,2,2048]{2,1,0:T(2,128)(2,1)S(1)}, u32[]{:S(2)}, u32[]{:S(2)}) async-start(bf16[16,2,2048]{2,1,0:T(2,128)(2,1)} %reshape.239), calls=%async_computation.3 | async-start | bytes 262144 | tf_op jit(solution)/shard_map/all_to_all | solution.py:177
  558.0 0.3 select_reduce_fusion.2
  558.4 8.8 %all-to-all-done.2 = bf16[16,2,2048]{2,1,0:T(2,128)(2,1)S(1)} async-done(((bf16[16,2,2048]{2,1,0:T(2,128)(2,1)}), bf16[16,2,2048]{2,1,0:T(2,128)(2,1)S(1)}, u32[]{:S(2)}, u32[]{:S(2)}) %all-to-all-start.2) | async-done | bytes 131104 | tf_op jit(solution)/shard_map/all_to_all | solution.py:177
  567.2 0.9 fusion
  (56 shorter events, 1.2 us)
Async XLA Ops:
  6.5 306.2 %copy-start = (bf16[1,256,2048]{2,1,0:T(8,128)(2,1)S(1)}, bf16[1,256,2048]{2,1,0:T(8,128)(2,1)}, u32[]{:S(2)}) copy-start(bf16[1,256,2048]{2,1,0:T(8,128)(2,1)} %param.31) | copy-start | bytes 3145732
  6.5 34.6 %copy-start.6 = (f32[256,2]{0,1:T(2,128)S(1)}, f32[256,2]{0,1:T(2,128)}, u32[]{:S(2)}) copy-start(f32[256,2]{0,1:T(2,128)} %param.18) | copy-start | bytes 6148
  6.5 34.4 %copy-start.3 = (bf16[256,128]{1,0:T(8,128)(2,1)S(1)}, bf16[256,128]{1,0:T(8,128)(2,1)}, u32[]{:S(2)}) copy-start(bf16[256,128]{1,0:T(8,128)(2,1)} %param.21) | copy-start | bytes 196612
  6.5 34.6 %copy-start.11 = (f32[2]{0:T(128)S(1)}, f32[2]{0:T(128)}, u32[]{:S(2)}) copy-start(f32[2]{0:T(128)} %param.22) | copy-start | bytes 28
  6.5 35.3 %copy-start.2 = (bf16[256,128]{1,0:T(8,128)(2,1)S(1)}, bf16[256,128]{1,0:T(8,128)(2,1)}, u32[]{:S(2)}) copy-start(bf16[256,128]{1,0:T(8,128)(2,1)} %param.17) | copy-start | bytes 196612
  6.5 96.8 %copy-start.8 = (f32[128]{0:T(128)S(1)}, f32[128]{0:T(128)}, u32[]{:S(2)}) copy-start(f32[128]{0:T(128)} %param.23) | copy-start | bytes 1540
  6.6 97.5 %copy-start.7 = (s32[8,2]{0,1:T(2,128)S(1)}, s32[8,2]{0,1:T(2,128)}, u32[]{:S(2)}) copy-start(s32[8,2]{0,1:T(2,128)} %param.28) | copy-start | bytes 196
  6.6 180.0 %copy-start.1 = (bf16[4096,64]{0,1:T(8,128)(2,1)S(1)}, bf16[4096,64]{0,1:T(8,128)(2,1)}, u32[]{:S(2)}) copy-start(bf16[4096,64]{0,1:T(8,128)(2,1)} %param.24) | copy-start | bytes 1572868
  6.6 180.0 %all-gather.6.cloned.1.call-start = ((), (), s32[]{:S(2)}) async-start(), calls=%async_computation.6 | async-start | bytes 2162688 | tf_op jit(solution)/shard_map/all_gather | solution.py:148
  38.3 165.4 %copy-start.4 = (bf16[8,2048]{1,0:T(8,128)(2,1)S(1)}, bf16[8,2048]{1,0:T(8,128)(2,1)}, u32[]{:S(2)}) copy-start(bf16[8,2048]{1,0:T(8,128)(2,1)} %param.25) | copy-start | bytes 98308
  38.7 165.2 %copy-start.5 = (f32[2048]{0:T(1024)S(1)}, f32[2048]{0:T(1024)}, u32[]{:S(2)}) copy-start(f32[2048]{0:T(1024)} %param.26) | copy-start | bytes 24580
  189.8 13.7 %all-to-all-start = ((bf16[32,2,256]{2,1,0:T(2,128)(2,1)}), bf16[32,2,256]{2,1,0:T(2,128)(2,1)S(1)}, u32[]{:S(2)}, u32[]{:S(2)}) async-start(bf16[32,2,256]{2,1,0:T(2,128)(2,1)} %reshape.251), calls=%async_computation | async-start | bytes 65536 | tf_op jit(solution)/shard_map/all_to_all | solution.py:155
  194.7 106.3 %all-gather.4.cloned.1.call-start = ((), (), s32[]{:S(2)}) async-start(), calls=%async_computation.4 | async-start | bytes 4325376 | tf_op jit(solution)/shard_map/all_gather | solution.py:172
  227.1 81.2 %copy-start.9 = (bf16[1,2048,256]{2,1,0:T(8,128)(2,1)S(1)}, bf16[1,2048,256]{2,1,0:T(8,128)(2,1)}, u32[]{:S(2)}) copy-start(bf16[1,2048,256]{2,1,0:T(8,128)(2,1)} %param.29) | copy-start | bytes 3145732
  227.1 316.9 %reduce-scatter.2.cloned.1.call-start = ((), (), s32[]{:S(2)}) async-start(), calls=%async_computation.5 | async-start | bytes 4325376 | tf_op jit(solution)/shard_map/reduce_scatter | solution.py:48
  321.9 236.1 %copy-start.10 = (f32[2048,16]{0,1:T(8,128)S(1)}, f32[2048,16]{0,1:T(8,128)}, u32[]{:S(2)}) copy-start(f32[2048,16]{0,1:T(8,128)} %param.27) | copy-start | bytes 393220
  545.6 21.6 %all-to-all-start.2 = ((bf16[16,2,2048]{2,1,0:T(2,128)(2,1)}), bf16[16,2,2048]{2,1,0:T(2,128)(2,1)S(1)}, u32[]{:S(2)}, u32[]{:S(2)}) async-start(bf16[16,2,2048]{2,1,0:T(2,128)(2,1)} %reshape.239), calls=%async_computation.3 | async-start | bytes 262144 | tf_op jit(solution)/shard_map/all_to_all | solution.py:177
Sparse Core Ops, SparseCore 0:
  104.2 82.3 all-gather.5
  227.2 73.7 all-gather.3
  322.0 221.9 reduce-scatter.1
where the time goes:
time: 575 us
  waiting for transfers between devices  395 us (69%)
  blocking collectives  110 us (19%)
  matrix products  20.9 us (4%)
  starting transfers between devices  17.4 us (3%)
  between operations  13.4 us (2%)
  local copies, waits for them, and re-layouts  13.3 us (2%)
    reduce_scatter x1, waiting for transfers between devices, sum_by_axis(): total = lax.psum_scatter(total, axes, scatter_dimension=0, tiled=True)  222 us
    all_gather x1, waiting for transfers between devices, shards(): gathered = lax.all_gather(mixed_rows, DEV, axis=0)  81.8 us
    all_gather x1, waiting for transfers between devices, shards(): lax.all_gather(arrived, DEV, axis=0, tiled=True).reshape(-1, model_dim)  73.9 us
    psum x1, blocking collectives, shards(): squares = lax.psum(jnp.sum(gated_out * gated_out, axis=1), DEV)  61.3 us
    all_gather x1, blocking collectives, side_by_side(): lax.all_gather(both, axis, axis=dim, tiled=True)  26 us
    all_to_all x1, blocking collectives, shards(): lax.all_to_all(outgoing, 'grp', split_axis=0, concat_axis=0, tiled=True)  22.8 us
    all_to_all x1, starting transfers between devices, shards(): lax.all_to_all(summed.astype(jnp.bfloat16).reshape(experts, slot_cap, mod...  12.4 us
  transfers between devices with their start and end apart: 5, of which 5 were waited for; matrix products, arithmetic and copies ran while one was open for 0% of the time, Pallas kernels for 0%

commit v1 on v0

--- a/solution.py
+++ b/solution.py
@@ -141,7 +141,8 @@
     gated_out = ssm_out.reshape(tok_rows, head_count * head_width) * jax.nn.silu(
         gate_input.astype(jnp.float32)
     )
-    squares = lax.psum(jnp.sum(gated_out * gated_out, axis=1), DEV)
+    one_axis = lax.psum(jnp.sum(gated_out * gated_out, axis=1), "dev_0")
+    squares = lax.psum(one_axis, "dev_1")
     mixed_rows = (
         gated_out * lax.rsqrt(squares[:, None] / inner_dim + EPSILON) * norm_gain[None, :]
     ).astype(jnp.bfloat16)

time: 575 us -> 531 us (0.923)
  blocking collectives: 110 us -> 71.3 us
  waiting for transfers between devices: 395 us -> 389 us
    psum x1 -> x2, blocking collectives: 61.3 us -> 22.6 us  [the longest x1 14.1 us: shards(): squares = lax.psum(one_axis, 'dev_1')]
where the time goes in v1:
time: 531 us; the launch traced here: 530 us
  waiting for transfers between devices  389 us (73%)
  blocking collectives  71.3 us (13%)
  matrix products  20.9 us (4%)
  starting transfers between devices  17.5 us (3%)
  between operations  13.4 us (3%)
  local copies, waits for them, and re-layouts  13.3 us (3%)
    reduce_scatter x1, waiting for transfers between devices, sum_by_axis(): total = lax.psum_scatter(total, axes, scatter_dimension=0, tiled=True)  222 us
    all_gather x1, waiting for transfers between devices, shards(): gathered = lax.all_gather(mixed_rows, DEV, axis=0)  76.1 us
    all_gather x1, waiting for transfers between devices, shards(): lax.all_gather(arrived, DEV, axis=0, tiled=True).reshape(-1, model_dim)  73.9 us
    all_gather x1, blocking collectives, side_by_side(): lax.all_gather(both, axis, axis=dim, tiled=True)  26 us
    all_to_all x1, blocking collectives, shards(): lax.all_to_all(outgoing, 'grp', split_axis=0, concat_axis=0, tiled=True)  22.8 us
    psum x1, blocking collectives, shards(): squares = lax.psum(one_axis, 'dev_1')  14.1 us
    all_to_all x1, starting transfers between devices, shards(): lax.all_to_all(summed.astype(jnp.bfloat16).reshape(experts, slot_cap, mod...  12.4 us
  transfers between devices with their start and end apart: 5, of which 5 were waited for; matrix products, arithmetic and copies ran while one was open for 0% of the time, Pallas kernels for 0%

profile of v1, /device:TPU:1, one launch (start us, length us, event | category | flops | bytes accessed | tf_op | source)
XLA Modules:
  0.0 530.2 jit_solution(4325999446206772022)
XLA Ops:
  6.6 0.9 negate_bitcast_fusion
  7.5 0.6 reduce-window.6
  8.1 0.2 slice_reduce_fusion
  8.3 0.2 reduce-window.9
  8.5 0.2 slice_reduce_fusion.1
  8.8 0.8 fusion.58
  9.5 0.9 copy.61
  10.5 1.0 convolution_convert_fusion.2
  11.6 0.1 pad_maximum_fusion
  11.7 26.0 %all_gather.12 = bf16[16,2,8193]{2,1,0:T(2,128)(2,1)S(1)} all-gather(bf16[1,2,8193]{2,1,0:T(2,128)(2,1)S(1)} %pad_maximum_fusion), channel_id=1, replica_groups=mesh['grp'=16,'dev_0'=4,'dev_1'=8] {'grp'}, dimensions={0}, use_global_device_ids=true | all-gather | bytes 557124 | tf_op jit(solution)/shard_map/all_gather | solution.py:16
  37.6 0.7 slice.40
  38.4 0.1 copy.76
  38.5 0.1 copy.64
  38.6 0.1 select_reduce_fusion.1
  38.9 0.4 reshape.234
  39.3 1.1 fusion.59
  40.3 0.6 fusion.18
  40.9 0.2 fusion.4
  41.2 0.6 fusion.3
  41.8 0.1 copy.66
  41.9 0.1 multiply_reduce_fusion
  42.0 8.5 %psum.14 = f32[256]{0:T(256)S(1)} all-reduce(f32[256]{0:T(256)S(1)} %multiply_reduce_fusion), channel_id=1, replica_groups=mesh['grp'=16,'dev_0'=4,'dev_1'=8] {'dev_0'}, use_global_device_ids=true, to_apply=%region_5.6 | all-reduce | flops 256 | bytes 2048 | tf_op jit(solution)/shard_map/psum | solution.py:144
  50.5 14.1 %psum.15 = f32[256]{0:T(256)S(1)} all-reduce(f32[256]{0:T(256)S(1)} %psum.14), channel_id=1, replica_groups=mesh['grp'=16,'dev_0'=4,'dev_1'=8] {'dev_1'}, use_global_device_ids=true, to_apply=%region_6.7 | all-reduce | flops 256 | bytes 2048 | tf_op jit(solution)/shard_map/psum | solution.py:145
  64.6 0.7 multiply_convert_fusion
  65.7 0.2 select_reduce_fusion
  66.0 0.1 copy.72
  66.0 76.1 %all-gather.6.cloned.1.call-done = bf16[8192,128]{1,0:T(8,128)(2,1)} async-done(((bf16[256,128]{1,0:T(8,128)(2,1)}), bf16[8192,128]{1,0:T(8,128)(2,1)}) %all-gather.6.cloned.1.call-update) | async-done | bytes 2097168 | tf_op jit(solution)/shard_map/all_gather | solution.py:149
  142.2 2.3 fusion.5
  144.5 0.1 copy.68
  144.6 0.7 reshape.251
  145.4 4.9 all-to-all-start
  150.5 8.6 %all-to-all-done = bf16[32,2,256]{2,1,0:T(2,128)(2,1)S(1)} async-done(((bf16[32,2,256]{2,1,0:T(2,128)(2,1)}), bf16[32,2,256]{2,1,0:T(2,128)(2,1)S(1)}, u32[]{:S(2)}, u32[]{:S(2)}) %all-to-all-start) | async-done | bytes 32800 | tf_op jit(solution)/shard_map/all_to_all | solution.py:156
  159.1 0.1 reshape.252
  159.3 0.1 reshape.242
  159.4 0.1 fusion.37
  159.5 0.2 convolution_convert_fusion.1
  159.8 0.1 reshape.237
  159.9 22.8 %all_to_all.23 = bf16[16,2,2048]{2,1,0:T(2,128)(2,1)} all-to-all(bf16[16,2,2048]{2,1,0:T(2,128)(2,1)S(1)} %reshape.237), channel_id=1, replica_groups=mesh['grp'=16,'dev_0'=4,'dev_1'=8] {'grp'}, dimensions={0} | all-to-all | bytes 262144 | tf_op jit(solution)/shard_map/all_to_all | solution.py:172
  182.7 73.9 %all-gather.4.cloned.1.call-done = bf16[512,2,2048]{2,1,0:T(2,128)(2,1)} async-done(((bf16[16,2,2048]{2,1,0:T(2,128)(2,1)}), bf16[512,2,2048]{2,1,0:T(2,128)(2,1)}) %all-gather.4.cloned.1.call-update) | async-done | bytes 4194320 | tf_op jit(solution)/shard_map/all_gather | solution.py:173
  256.6 7.2 %reshape.238 = bf16[1024,2048]{1,0:T(8,128)(2,1)} reshape(bf16[512,2,2048]{2,1,0:T(2,128)(2,1)} %all-gather.4.cloned.1.call-done) | data formatting | bytes 8388608 | tf_op jit(solution)/shard_map/reshape | solution.py:173
  263.8 4.5 fusion.9
  268.3 9.1 %convolution_convert_fusion = bf16[1024,2048]{1,0:T(8,128)(2,1)} fusion(bf16[1024,2048]{1,0:T(8,128)(2,1)} %reshape.238, bf16[1,256,2048]{2,1,0:T(8,128)(2,1)S(1)} %copy-done, bf16[1,2048,256]{2,1,0:T(8,128)(2,1)} %param.30, f32[1024,256]{1,0:T(8,128)} %fusion.9), kind=kOutput, calls=%fused_computation | convolution fusion | flops 2151153664 | bytes 11534336 | tf_op jit(solution)/shard_map/dot_general | solution.py:177
  277.5 222.0 %reduce-scatter.2.cloned.1.call-done = bf16[32,2048]{1,0:T(8,128)(2,1)} async-done(((bf16[1024,2048]{1,0:T(8,128)(2,1)}), bf16[32,2048]{1,0:T(8,128)(2,1)}) %reduce-scatter.2.cloned.1.call-update) | async-done | bytes 131088 | tf_op jit(solution)/shard_map/reduce_scatter | solution.py:48
  499.5 1.7 reshape.239
  501.2 12.4 %all-to-all-start.2 = ((bf16[16,2,2048]{2,1,0:T(2,128)(2,1)}), bf16[16,2,2048]{2,1,0:T(2,128)(2,1)S(1)}, u32[]{:S(2)}, u32[]{:S(2)}) async-start(bf16[16,2,2048]{2,1,0:T(2,128)(2,1)} %reshape.239), calls=%async_computation.3 | async-start | bytes 262144 | tf_op jit(solution)/shard_map/all_to_all | solution.py:178
  513.6 0.3 select_reduce_fusion.2
  513.9 8.8 %all-to-all-done.2 = bf16[16,2,2048]{2,1,0:T(2,128)(2,1)S(1)} async-done(((bf16[16,2,2048]{2,1,0:T(2,128)(2,1)}), bf16[16,2,2048]{2,1,0:T(2,128)(2,1)S(1)}, u32[]{:S(2)}, u32[]{:S(2)}) %all-to-all-start.2) | async-done | bytes 131104 | tf_op jit(solution)/shard_map/all_to_all | solution.py:178
  522.8 0.9 fusion
  (57 shorter events, 1.3 us)
Async XLA Ops:
  6.5 261.8 %copy-start = (bf16[1,256,2048]{2,1,0:T(8,128)(2,1)S(1)}, bf16[1,256,2048]{2,1,0:T(8,128)(2,1)}, u32[]{:S(2)}) copy-start(bf16[1,256,2048]{2,1,0:T(8,128)(2,1)} %param.31) | copy-start | bytes 3145732
  6.5 34.6 %copy-start.6 = (f32[256,2]{0,1:T(2,128)S(1)}, f32[256,2]{0,1:T(2,128)}, u32[]{:S(2)}) copy-start(f32[256,2]{0,1:T(2,128)} %param.18) | copy-start | bytes 6148
  6.5 34.4 %copy-start.3 = (bf16[256,128]{1,0:T(8,128)(2,1)S(1)}, bf16[256,128]{1,0:T(8,128)(2,1)}, u32[]{:S(2)}) copy-start(bf16[256,128]{1,0:T(8,128)(2,1)} %param.21) | copy-start | bytes 196612
  6.5 34.6 %copy-start.11 = (f32[2]{0:T(128)S(1)}, f32[2]{0:T(128)}, u32[]{:S(2)}) copy-start(f32[2]{0:T(128)} %param.22) | copy-start | bytes 28
  6.5 35.3 %copy-start.2 = (bf16[256,128]{1,0:T(8,128)(2,1)S(1)}, bf16[256,128]{1,0:T(8,128)(2,1)}, u32[]{:S(2)}) copy-start(bf16[256,128]{1,0:T(8,128)(2,1)} %param.17) | copy-start | bytes 196612
  6.5 58.1 %copy-start.8 = (f32[128]{0:T(128)S(1)}, f32[128]{0:T(128)}, u32[]{:S(2)}) copy-start(f32[128]{0:T(128)} %param.23) | copy-start | bytes 1540
  6.6 58.8 %copy-start.7 = (s32[8,2]{0,1:T(2,128)S(1)}, s32[8,2]{0,1:T(2,128)}, u32[]{:S(2)}) copy-start(s32[8,2]{0,1:T(2,128)} %param.28) | copy-start | bytes 196
  6.6 135.6 %copy-start.1 = (bf16[4096,64]{0,1:T(8,128)(2,1)S(1)}, bf16[4096,64]{0,1:T(8,128)(2,1)}, u32[]{:S(2)}) copy-start(bf16[4096,64]{0,1:T(8,128)(2,1)} %param.24) | copy-start | bytes 1572868
  6.6 135.6 %all-gather.6.cloned.1.call-start = ((), (), s32[]{:S(2)}) async-start(), calls=%async_computation.6 | async-start | bytes 2162688 | tf_op jit(solution)/shard_map/all_gather | solution.py:149
  38.3 121.0 %copy-start.4 = (bf16[8,2048]{1,0:T(8,128)(2,1)S(1)}, bf16[8,2048]{1,0:T(8,128)(2,1)}, u32[]{:S(2)}) copy-start(bf16[8,2048]{1,0:T(8,128)(2,1)} %param.25) | copy-start | bytes 98308
  38.7 120.8 %copy-start.5 = (f32[2048]{0:T(1024)S(1)}, f32[2048]{0:T(1024)}, u32[]{:S(2)}) copy-start(f32[2048]{0:T(1024)} %param.26) | copy-start | bytes 24580
  145.4 13.7 %all-to-all-start = ((bf16[32,2,256]{2,1,0:T(2,128)(2,1)}), bf16[32,2,256]{2,1,0:T(2,128)(2,1)S(1)}, u32[]{:S(2)}, u32[]{:S(2)}) async-start(bf16[32,2,256]{2,1,0:T(2,128)(2,1)} %reshape.251), calls=%async_computation | async-start | bytes 65536 | tf_op jit(solution)/shard_map/all_to_all | solution.py:156
  150.3 106.3 %all-gather.4.cloned.1.call-start = ((), (), s32[]{:S(2)}) async-start(), calls=%async_computation.4 | async-start | bytes 4325376 | tf_op jit(solution)/shard_map/all_gather | solution.py:173
  182.7 81.2 %copy-start.9 = (bf16[1,2048,256]{2,1,0:T(8,128)(2,1)S(1)}, bf16[1,2048,256]{2,1,0:T(8,128)(2,1)}, u32[]{:S(2)}) copy-start(bf16[1,2048,256]{2,1,0:T(8,128)(2,1)} %param.29) | copy-start | bytes 3145732
  182.7 316.8 %reduce-scatter.2.cloned.1.call-start = ((), (), s32[]{:S(2)}) async-start(), calls=%async_computation.5 | async-start | bytes 4325376 | tf_op jit(solution)/shard_map/reduce_scatter | solution.py:48
  277.4 236.1 %copy-start.10 = (f32[2048,16]{0,1:T(8,128)S(1)}, f32[2048,16]{0,1:T(8,128)}, u32[]{:S(2)}) copy-start(f32[2048,16]{0,1:T(8,128)} %param.27) | copy-start | bytes 393220
  501.2 21.6 %all-to-all-start.2 = ((bf16[16,2,2048]{2,1,0:T(2,128)(2,1)}), bf16[16,2,2048]{2,1,0:T(2,128)(2,1)S(1)}, u32[]{:S(2)}, u32[]{:S(2)}) async-start(bf16[16,2,2048]{2,1,0:T(2,128)(2,1)} %reshape.239), calls=%async_computation.3 | async-start | bytes 262144 | tf_op jit(solution)/shard_map/all_to_all | solution.py:178
Sparse Core Ops, SparseCore 0:
  65.5 76.6 all-gather.5
  182.8 73.7 all-gather.3
  277.6 221.8 reduce-scatter.1
